TPU v7x, 256 devices: a whole 4x4x8 slice. The times are simulated.
256 devices in a mesh: dp: 32 (over x, z_hi, core), tensor: 8 (over y, z_lo).
Axes of the slice: x: 4, y: 4, z: 8 (z_hi: 4, z_lo: 2; z = z_hi * 2 + z_lo), core: 2. Of those that a mesh axis runs over, the one named last changes fastest.
Arguments:
- stream: bfloat16 [64, 430, 2048], P('dp', None, 'tensor'), may hold values from -3 to 3
- normed: bfloat16 [64, 430, 2048], P('dp'), may hold values from -6 to 6
- query_weight: bfloat16 [2048, 2048], P(None, 'tensor'), as said below
- key_weight: bfloat16 [2048, 2048], P(None, 'tensor'), as said below
- value_weight: bfloat16 [2048, 2048], P(None, 'tensor'), may hold values from -0.125 to 0.125
- out_weight: bfloat16 [2048, 2048], P('tensor'), may hold values from -0.125 to 0.125
- norm_gain: bfloat16 [2048], P('tensor'), may hold values from 0.099609375 to 1.8984375
- proj_weight: bfloat16 [2048, 1024], P('tensor'), may hold values from -0.125 to 0.125
- images: bfloat16 [64, 1024], P('dp'), may hold values from -6 to 6
Outputs:
- mean_loss: float32 [], replicated
- grad_normed: bfloat16 [64, 430, 2048], P('dp', None, 'tensor')
- grad_query: float32 [2048, 2048], P('dp', 'tensor')
- grad_key: float32 [2048, 2048], P('dp', 'tensor')
- grad_value: float32 [2048, 2048], P('dp', 'tensor')
- grad_out: float32 [2048, 2048], P('tensor', 'dp')
- grad_proj: float32 [2048, 1024], P('tensor', 'dp')
Inputs may be any that keep to these rules, and one draw needn't show every extreme that they name: `query_weight`: query projection entries, independent draws of order 2048^-0.5. `key_weight`: key projection entries, of order 2048^-0.5, in some heads up to about sixteen times that, possibly aligned with the query projection.
All inputs are finite; a program needn't handle non-finite values.
Results may differ from a plain program's by a relative error of at most 0.02.
Values may be sent and summed in bfloat16 or wider, within the bound.
No kernel may reach another device: no remote copies, remote signals or barrier semaphores. Data moves between devices by JAX's collectives and lax.ppermute only.
A program may use at most 128 MiB of HBM per device.

v0:
```python
import jax
import jax.numpy as jnp
from jax import lax
from jax.sharding import PartitionSpec as P

D = 2048
H = 16
SCALE_LOGIT = 14.0
GRAD_SCALE = 256.0
EPSILON = 1e-05
HIGH = lax.Precision.HIGHEST


def project(inputs, weight):
    return jnp.einsum("bld,dc->blc", inputs, weight, preferred_element_type=jnp.float32).astype(
        jnp.bfloat16
    )


def split_heads(values, head_size):
    return values.reshape(values.shape[0], values.shape[1], values.shape[2] // head_size, head_size)


def local(
    stream,
    normed,
    query_weight,
    key_weight,
    value_weight,
    out_weight,
    norm_gain,
    proj_weight,
    images,
):
    seq_count = normed.shape[0]
    length = normed.shape[1]
    col_count = query_weight.shape[1]
    feat_share = stream.shape[2]
    head_size = D // H
    scale_head = head_size ** (-0.5)
    queries = split_heads(project(normed, query_weight), head_size)
    keys_all = split_heads(project(normed, key_weight), head_size)
    values_all = split_heads(project(normed, value_weight), head_size)
    scores = (
        jnp.einsum("bqhd,bkhd->bhqk", queries, keys_all, preferred_element_type=jnp.float32)
        * scale_head
    )
    row_max = jnp.max(scores, axis=-1, keepdims=True)
    exp_scores = jnp.exp(scores - row_max)
    attn_prob = exp_scores / jnp.sum(exp_scores, axis=-1, keepdims=True)
    attn_half = attn_prob.astype(jnp.bfloat16)
    heads_out = jnp.einsum(
        "bhqk,bkhd->bqhd", attn_half, values_all, preferred_element_type=jnp.float32
    )
    head_concat = heads_out.astype(jnp.bfloat16).reshape(seq_count, length, col_count)
    partial_value = jnp.einsum(
        "blc,cd->bld", head_concat, out_weight, preferred_element_type=jnp.float32
    )
    summed = lax.psum(partial_value.astype(jnp.bfloat16), "tensor").astype(jnp.float32)
    attended = lax.dynamic_slice_in_dim(
        summed, lax.axis_index("tensor") * feat_share, feat_share, 2
    )
    residual = stream.astype(jnp.float32) + attended
    center = lax.psum(jnp.sum(residual, axis=-1), "tensor") / D
    offset = residual - center[..., None]
    variance = lax.psum(jnp.sum(offset * offset, axis=-1), "tensor") / D
    inv_std = lax.rsqrt(variance + EPSILON)[..., None]
    normal_feat = (residual - center[..., None]) * inv_std
    gain_float = norm_gain.astype(jnp.float32)
    pooled = jnp.mean(normal_feat * gain_float, axis=1).astype(jnp.bfloat16)
    embedded = lax.psum(jnp.dot(pooled, proj_weight, preferred_element_type=jnp.float32), "tensor")
    embed_norm = jnp.sqrt(jnp.sum(embedded * embedded, axis=-1, keepdims=True) + EPSILON)
    spectra = embedded / embed_norm
    gathered = lax.all_gather(images, "dp", axis=0, tiled=True).astype(jnp.float32)
    image_unit = gathered / jnp.sqrt(jnp.sum(gathered * gathered, axis=-1, keepdims=True) + EPSILON)
    logits = SCALE_LOGIT * jnp.dot(spectra, image_unit.T, precision=HIGH)
    own_start = lax.axis_index("dp") * seq_count
    columns = jnp.arange(logits.shape[1], dtype=jnp.int32)
    own_rows = own_start + jnp.arange(seq_count, dtype=jnp.int32)
    matches = (columns[None, :] == own_rows[:, None]).astype(jnp.float32)
    exp_logits = jnp.exp(logits)
    row_lse = jnp.log(jnp.sum(exp_logits, axis=1))
    diagonal = jnp.sum(logits * matches, axis=1)
    local_loss = 0.5 * jnp.sum(row_lse) - jnp.sum(diagonal)
    col_total, loss_sum = lax.psum((jnp.sum(exp_logits, axis=0), local_loss), "dp")
    col_lse = jnp.log(col_total)
    mean_loss = (loss_sum + 0.5 * jnp.sum(col_lse)) / logits.shape[1]
    grad_logits = GRAD_SCALE * (
        0.5 * jnp.exp(logits - row_lse[:, None])
        + 0.5 * jnp.exp(logits - col_lse[None, :])
        - matches
    )
    grad_spec = SCALE_LOGIT * jnp.dot(grad_logits, image_unit, precision=HIGH)
    radial = jnp.sum(spectra * grad_spec, axis=-1, keepdims=True)
    grad_embed = ((grad_spec - spectra * radial) / embed_norm).astype(jnp.bfloat16)
    grad_proj = lax.dot_general(
        pooled, grad_embed, (((0,), (0,)), ((), ())), preferred_element_type=jnp.float32
    )
    grad_pooled = lax.dot_general(
        grad_embed, proj_weight, (((1,), (1,)), ((), ())), preferred_element_type=jnp.float32
    )
    grad_normal = jnp.broadcast_to(grad_pooled[:, None, :] / length, normal_feat.shape) * gain_float
    mean_one, mean_two = lax.psum(
        (jnp.sum(grad_normal, axis=-1), jnp.sum(grad_normal * normal_feat, axis=-1)), "tensor"
    )
    grad_resid = (
        inv_std * (grad_normal - mean_one[..., None] / D - normal_feat * (mean_two[..., None] / D))
    ).astype(jnp.bfloat16)
    piece_rows = lax.all_gather(grad_resid, "tensor", axis=2, tiled=True)
    grad_heads = jnp.einsum(
        "blw,cw->blc", piece_rows, out_weight, preferred_element_type=jnp.float32
    )
    update = jnp.einsum("blc,blw->cw", head_concat, piece_rows, preferred_element_type=jnp.float32)
    grad_out = update
    grad_heads, grad_out = (grad_heads, grad_out)
    grad_heads = split_heads(grad_heads.astype(jnp.bfloat16), head_size)
    grad_probs = jnp.einsum(
        "bqhd,bkhd->bhqk", grad_heads, values_all, preferred_element_type=jnp.float32
    )
    row_dot = jnp.sum(attn_prob * grad_probs, axis=-1, keepdims=True)
    grad_scores = (attn_prob * (grad_probs - row_dot) * scale_head).astype(jnp.bfloat16)
    grad_q = (
        jnp.einsum("bhqk,bkhd->bqhd", grad_scores, keys_all, preferred_element_type=jnp.float32)
        .astype(jnp.bfloat16)
        .reshape(seq_count, length, col_count)
    )
    grad_k = (
        jnp.einsum("bhqk,bqhd->bkhd", grad_scores, queries, preferred_element_type=jnp.float32)
        .astype(jnp.bfloat16)
        .reshape(seq_count, length, col_count)
    )
    grad_v = (
        jnp.einsum("bhqk,bqhd->bkhd", attn_half, grad_heads, preferred_element_type=jnp.float32)
        .astype(jnp.bfloat16)
        .reshape(seq_count, length, col_count)
    )
    back_input = jnp.einsum("blc,dc->bld", grad_q, query_weight, preferred_element_type=jnp.float32)
    back_input = back_input + jnp.einsum(
        "blc,dc->bld", grad_k, key_weight, preferred_element_type=jnp.float32
    )
    back_input = back_input + jnp.einsum(
        "blc,dc->bld", grad_v, value_weight, preferred_element_type=jnp.float32
    )
    grad_normed = lax.psum_scatter(
        back_input.astype(jnp.bfloat16), "tensor", scatter_dimension=2, tiled=True
    )
    grad_query = jnp.einsum("bld,blc->dc", normed, grad_q, preferred_element_type=jnp.float32)
    grad_key = jnp.einsum("bld,blc->dc", normed, grad_k, preferred_element_type=jnp.float32)
    grad_value = jnp.einsum("bld,blc->dc", normed, grad_v, preferred_element_type=jnp.float32)
    reduced = (
        lax.psum_scatter(
            grad_query.astype(jnp.bfloat16), "dp", scatter_dimension=0, tiled=True
        ).astype(jnp.float32),
        lax.psum_scatter(
            grad_key.astype(jnp.bfloat16), "dp", scatter_dimension=0, tiled=True
        ).astype(jnp.float32),
        lax.psum_scatter(
            grad_value.astype(jnp.bfloat16), "dp", scatter_dimension=0, tiled=True
        ).astype(jnp.float32),
        lax.psum_scatter(
            grad_out.astype(jnp.bfloat16), "dp", scatter_dimension=1, tiled=True
        ).astype(jnp.float32),
        lax.psum_scatter(
            grad_proj.astype(jnp.bfloat16), "dp", scatter_dimension=1, tiled=True
        ).astype(jnp.float32),
    )
    return (mean_loss, grad_normed, reduced[0], reduced[1], reduced[2], reduced[3], reduced[4])


def solution(mesh):
    return jax.shard_map(
        local,
        mesh=mesh,
        in_specs=(
            P("dp", None, "tensor"),
            P("dp", None, None),
            P(None, "tensor"),
            P(None, "tensor"),
            P(None, "tensor"),
            P("tensor", None),
            P("tensor"),
            P("tensor", None),
            P("dp", None),
        ),
        out_specs=(
            P(),
            P("dp", None, "tensor"),
            P("dp", "tensor"),
            P("dp", "tensor"),
            P("dp", "tensor"),
            P("tensor", "dp"),
            P("tensor", "dp"),
        ),
        check_vma=False,
    )
```

profile of v0, /device:TPU:1, one launch (start us, length us, event | category | flops | bytes accessed | tf_op | source)
XLA Modules:
  0.0 972.7 jit_solution(16875496119188521870)
XLA Ops:
  7.2 4.5 fusion.42
  16.0 4.3 fusion.39
  24.0 4.7 fusion.48
  32.5 50.5 %all-gather = bf16[32,2,1024]{2,1,0:T(2,128)(2,1)S(1)} all-gather(bf16[1,2,1024]{2,1,0:T(2,128)(2,1)S(1)} %bitcast.72), channel_id=1, replica_groups=mesh['dp'=32,'tensor'=8] {'dp'}, dimensions={0}, use_global_device_ids=true | all-gather | bytes 135168 | tf_op jit(solution)/shard_map/all_gather | solution.py:74
  83.2 117.2 %all-reduce.4.cloned.1.call-done = bf16[2,430,2048]{2,1,0:T(8,128)(2,1)} async-done(((bf16[2,430,2048]{2,1,0:T(8,128)(2,1)}), bf16[2,430,2048]{2,1,0:T(8,128)(2,1)}) %all-reduce.4.cloned.1.call-update) | async-done | bytes 3522576 | tf_op jit(solution)/shard_map/psum | solution.py:59
  201.6 12.8 %psum.57 = f32[2,430]{1,0:T(2,128)S(1)} all-reduce(f32[2,430]{1,0:T(2,128)S(1)} %fusion.73), channel_id=1, replica_groups=mesh['dp'=32,'tensor'=8] {'tensor'}, use_global_device_ids=true, to_apply=%region_4.0 | all-reduce | flops 860 | bytes 6880 | tf_op jit(solution)/shard_map/psum | solution.py:64
  215.8 13.8 %psum.58 = f32[2,430]{1,0:T(2,128)S(1)} all-reduce(f32[2,430]{1,0:T(2,128)S(1)} %multiply_reduce_fusion.4), channel_id=1, replica_groups=mesh['dp'=32,'tensor'=8] {'tensor'}, use_global_device_ids=true, to_apply=%region_6.0 | all-reduce | flops 860 | bytes 6880 | tf_op jit(solution)/shard_map/psum | solution.py:66
  231.2 13.3 %psum.59 = f32[2,1024]{1,0:T(2,128)S(1)} all-reduce(f32[2,1024]{1,0:T(2,128)S(1)} %fusion.102), channel_id=1, replica_groups=mesh['dp'=32,'tensor'=8] {'tensor'}, use_global_device_ids=true, to_apply=%region_8.0 | all-reduce | flops 2048 | bytes 16384 | tf_op jit(solution)/shard_map/psum | solution.py:71
  247.5 83.0 %all-reduce = (f32[64]{0:T(128)S(1)}, f32[]{:T(128)}) all-reduce(f32[64]{0:T(128)S(1)} %get-tuple-element.30, f32[]{:T(128)S(6)} %sub.68), channel_id=1, replica_groups=mesh['dp'=32,'tensor'=8] {'dp'}, use_global_device_ids=true, to_apply=%region_16.0 | all-reduce | flops 65 | bytes 520 | tf_op jit(solution)/shard_map/psum | solution.py:85
  333.5 13.0 %all-reduce.1 = (f32[2,430]{1,0:T(2,128)S(1)}, f32[2,430]{1,0:T(2,128)S(1)}) all-reduce(f32[2,430]{1,0:T(2,128)S(1)} %get-tuple-element.29, f32[2,430]{1,0:T(2,128)S(1)} %get-tuple-element.28), channel_id=1, replica_groups=mesh['dp'=32,'tensor'=8] {'tensor'}, use_global_device_ids=true, to_apply=%region_22.0 | all-reduce | flops 1720 | bytes 13760 | tf_op jit(solution)/shard_map/psum | solution.py:103
  350.3 73.9 %all-gather.3.cloned.1.call-done = bf16[2,430,2048]{2,1,0:T(8,128)(2,1)} async-done(((bf16[2,430,256]{2,1,0:T(8,128)(2,1)}), bf16[2,430,2048]{2,1,0:T(8,128)(2,1)}) %all-gather.3.cloned.1.call-update) | async-done | bytes 3522576 | tf_op jit(solution)/shard_map/all_gather | solution.py:109
  427.5 4.5 fusion.49
  432.6 4.4 fusion.12
  442.2 6.6 fusion.50
  449.5 4.4 fusion.13
  455.3 7.0 fusion.53
  462.9 4.4 fusion.14
  468.8 4.9 fusion.11
  480.7 35.0 %reduce-scatter.17.cloned.1.call-done = bf16[256,32]{0,1:T(8,128)(2,1)} async-done(((bf16[256,1024]{0,1:T(8,128)(2,1)}), bf16[256,32]{0,1:T(8,128)(2,1)}) %reduce-scatter.17.cloned.1.call-update) | async-done | bytes 16400 | tf_op jit(solution)/shard_map/reduce_scatter | solution.py:163
  517.1 89.3 %reduce-scatter.23.cloned.1.call-done = bf16[64,256]{1,0:T(8,128)(2,1)} async-done(((bf16[2048,256]{1,0:T(8,128)(2,1)}), bf16[64,256]{1,0:T(8,128)(2,1)}) %reduce-scatter.23.cloned.1.call-update) | async-done | bytes 32784
  608.0 89.1 %reduce-scatter.21.cloned.1.call-done = bf16[64,256]{1,0:T(8,128)(2,1)} async-done(((bf16[2048,256]{1,0:T(8,128)(2,1)}), bf16[64,256]{1,0:T(8,128)(2,1)}) %reduce-scatter.21.cloned.1.call-update) | async-done | bytes 32784
  698.7 89.1 %reduce-scatter.19.cloned.1.call-done = bf16[64,256]{1,0:T(8,128)(2,1)} async-done(((bf16[2048,256]{1,0:T(8,128)(2,1)}), bf16[64,256]{1,0:T(8,128)(2,1)}) %reduce-scatter.19.cloned.1.call-update) | async-done | bytes 32784
  789.4 89.2 %reduce-scatter.15.cloned.1.call-done = bf16[256,64]{0,1:T(8,128)(2,1)} async-done(((bf16[256,2048]{0,1:T(8,128)(2,1)}), bf16[256,64]{0,1:T(8,128)(2,1)}) %reduce-scatter.15.cloned.1.call-update) | async-done | bytes 32784 | tf_op jit(solution)/shard_map/reduce_scatter | solution.py:160
  880.0 82.3 %reduce-scatter.13.cloned.1.call-done = bf16[2,430,256]{2,1,0:T(8,128)(2,1)} async-done(((bf16[2,430,2048]{2,1,0:T(8,128)(2,1)}), bf16[2,430,256]{2,1,0:T(8,128)(2,1)}) %reduce-scatter.13.cloned.1.call-update) | async-done | bytes 440336 | tf_op jit(solution)/shard_map/reduce_scatter | solution.py:144
  (97 shorter events, 52.6 us)
Async XLA Ops:
  7.2 22.2 %copy-start = (bf16[256,2048]{1,0:T(8,128)(2,1)S(1)}, bf16[256,2048]{1,0:T(8,128)(2,1)}, u32[]{:S(2)}) copy-start(bf16[256,2048]{1,0:T(8,128)(2,1)} %param.14) | copy-start | bytes 3145732
  7.2 4.7 copy-start.7
  7.2 193.2 %all-reduce.4.cloned.1.call-start = ((), (), s32[]{:S(2)}) async-start(), calls=%async_computation.6 | async-start | bytes 7077888 | tf_op jit(solution)/shard_map/psum | solution.py:59
  20.5 3.5 copy-start.3
  21.2 2.8 copy-start.1
  29.3 3.0 copy-start.5
  29.4 3.1 copy-start.12
  29.4 3.1 copy-start.11
  29.4 171.0 %copy-start.2 = (bf16[2,430,256]{2,0,1:T(2,128)(2,1)S(1)}, bf16[2,430,256]{2,0,1:T(2,128)(2,1)}, u32[]{:S(2)}) copy-start(bf16[2,430,256]{2,0,1:T(2,128)(2,1)} %param.9) | copy-start | bytes 1320964
  32.4 198.6 %copy-start.10 = (bf16[256,1024]{1,0:T(8,128)(2,1)S(1)}, bf16[256,1024]{1,0:T(8,128)(2,1)}, u32[]{:S(2)}) copy-start(bf16[256,1024]{1,0:T(8,128)(2,1)} %param.16) | copy-start | bytes 1572868
  32.4 391.8 %all-gather.3.cloned.1.call-start = ((), (), s32[]{:S(2)}) async-start(), calls=%async_computation.7 | async-start | bytes 3981312 | tf_op jit(solution)/shard_map/all_gather | solution.py:109
  348.9 166.8 %reduce-scatter.17.cloned.1.call-start = ((), (), s32[]{:S(2)}) async-start(), calls=%async_computation.10 | async-start | bytes 540672 | tf_op jit(solution)/shard_map/reduce_scatter | solution.py:163
  350.2 256.2 %reduce-scatter.23.cloned.1.call-start = ((), (), s32[]{:S(2)}) async-start(), calls=%async_computation.13 | async-start | bytes 1081344
  427.5 4.5 copy-start.4
  438.4 258.7 %reduce-scatter.21.cloned.1.call-start = ((), (), s32[]{:S(2)}) async-start(), calls=%async_computation.12 | async-start | bytes 1081344
  455.3 332.5 %reduce-scatter.19.cloned.1.call-start = ((), (), s32[]{:S(2)}) async-start(), calls=%async_computation.11 | async-start | bytes 1081344
  468.7 5.2 copy-start.6
  468.7 409.9 %reduce-scatter.15.cloned.1.call-start = ((), (), s32[]{:S(2)}) async-start(), calls=%async_computation.9 | async-start | bytes 1081344 | tf_op jit(solution)/shard_map/reduce_scatter | solution.py:160
  473.7 488.7 %reduce-scatter.13.cloned.1.call-start = ((), (), s32[]{:S(2)}) async-start(), calls=%async_computation.8 | async-start | bytes 3981312 | tf_op jit(solution)/shard_map/reduce_scatter | solution.py:144
  474.0 1.2 copy-start.8
  475.2 1.2 copy-start.9
Sparse Core Ops, SparseCore 0:
  32.5 167.8 all-reduce.3
  349.0 75.1 all-gather.2
  427.9 87.7 reduce-scatter.16
  519.4 86.9 reduce-scatter.22
  610.0 87.0 reduce-scatter.20
  700.7 87.0 reduce-scatter.18
  791.6 87.0 reduce-scatter.14
  881.2 81.0 reduce-scatter.12
where the time goes:
time: 982 us; the launch traced here: 973 us
  waiting for transfers between devices  665 us (68%)
  blocking collectives  186 us (19%)
  matrix products  72.4 us (7%)
  between operations  18.5 us (2%)
  other arithmetic  15 us (2%)
  local copies, waits for them, and re-layouts  14.2 us (1%)
    unnamed x11, waiting for transfers between devices  268 us
    psum x1, waiting for transfers between devices, local(): lax.psum(partial_value.astype(jnp.bfloat16), 'tensor').astype(jnp.float32)  117 us
    reduce_scatter x1, waiting for transfers between devices, local(): lax.psum_scatter(grad_out.astype(jnp.bfloat16), 'dp', scatter_dimension=1...  89.2 us
    psum x1, blocking collectives, local(): lax.psum((jnp.sum(exp_logits, axis=0), local_loss), 'dp')  83 us
    reduce_scatter x1, waiting for transfers between devices, local(): lax.psum_scatter(back_input.astype(jnp.bfloat16), 'tensor', scatter_dimen...  82.3 us
    all_gather x1, waiting for transfers between devices, local(): piece_rows = lax.all_gather(grad_resid, 'tensor', axis=2, tiled=True)  73.9 us
    all_gather x1, blocking collectives, local(): lax.all_gather(images, 'dp', axis=0, tiled=True).astype(jnp.float32)  50.5 us
    reduce_scatter x1, waiting for transfers between devices, local(): lax.psum_scatter(grad_proj.astype(jnp.bfloat16), 'dp', scatter_dimension=...  35 us
  transfers between devices with their start and end apart: 8, of which 8 were waited for; matrix products, arithmetic and copies ran while one was open for 6% of the time, Pallas kernels for 0%

commit v1 on v0

--- a/solution.py
+++ b/solution.py
@@ -9,6 +9,11 @@
 GRAD_SCALE = 256.0
 EPSILON = 1e-05
 HIGH = lax.Precision.HIGHEST
+
+
+def pages_link(tile_in, axis_id):
+    finding = lax.all_gather(tile_in, axis_name=axis_id).sum(axis=0)
+    return finding
 
 
 def project(inputs, weight):
@@ -56,7 +61,7 @@
     partial_value = jnp.einsum(
         "blc,cd->bld", head_concat, out_weight, preferred_element_type=jnp.float32
     )
-    summed = lax.psum(partial_value.astype(jnp.bfloat16), "tensor").astype(jnp.float32)
+    summed = pages_link(partial_value.astype(jnp.bfloat16), "tensor").astype(jnp.float32)
     attended = lax.dynamic_slice_in_dim(
         summed, lax.axis_index("tensor") * feat_share, feat_share, 2
     )

time: 982 us -> 1380 us (1.41)
  waiting for transfers between devices: 665 us -> 1050 us
    all_gather x0 -> x1, waiting for transfers between devices: none -> 499 us  [pages_link(): finding = lax.all_gather(tile_in, axis_name=axis_id).sum(axis=0)]
    psum x1 -> x0, waiting for transfers between devices: 117 us -> none  [local(): lax.psum(partial_value.astype(jnp.bfloat16), 'tensor').astype(jnp.float32)]
  transfers between devices with their start and end apart: 8 -> 8, of which waited for: 8 -> 8; matrix products, arithmetic and copies ran while one was open for 6% -> 4% of each run, Pallas kernels for 0% -> 0%
where the time goes in v1:
time: 1380 us; the launch traced here: 1370 us
  waiting for transfers between devices  1050 us (76%)
  blocking collectives  188 us (14%)
  matrix products  70.7 us (5%)
  other arithmetic  28.4 us (2%)
  between operations  18.5 us (1%)
  local copies, waits for them, and re-layouts  16 us (1%)
    all_gather x1, waiting for transfers between devices, pages_link(): finding = lax.all_gather(tile_in, axis_name=axis_id).sum(axis=0)  499 us
    unnamed x11, waiting for transfers between devices  268 us
    reduce_scatter x1, waiting for transfers between devices, local(): lax.psum_scatter(grad_out.astype(jnp.bfloat16), 'dp', scatter_dimension=1...  89.2 us
    psum x1, blocking collectives, local(): lax.psum((jnp.sum(exp_logits, axis=0), local_loss), 'dp')  82.7 us
    reduce_scatter x1, waiting for transfers between devices, local(): lax.psum_scatter(back_input.astype(jnp.bfloat16), 'tensor', scatter_dimen...  82.3 us
    all_gather x1, waiting for transfers between devices, local(): piece_rows = lax.all_gather(grad_resid, 'tensor', axis=2, tiled=True)  74 us
    all_gather x1, blocking collectives, local(): lax.all_gather(images, 'dp', axis=0, tiled=True).astype(jnp.float32)  50.4 us
    reduce_scatter x1, waiting for transfers between devices, local(): lax.psum_scatter(grad_proj.astype(jnp.bfloat16), 'dp', scatter_dimension=...  36.6 us
  transfers between devices with their start and end apart: 8, of which 8 were waited for; matrix products, arithmetic and copies ran while one was open for 4% of the time, Pallas kernels for 0%

profile of v1, /device:TPU:1, one launch (start us, length us, event | category | flops | bytes accessed | tf_op | source)
XLA Modules:
  0.0 1370.2 jit_solution(9700599846185294531)
XLA Ops:
  7.2 4.5 fusion.42
  23.7 4.7 fusion.48
  32.1 50.4 %all-gather.1 = bf16[32,2,1024]{2,1,0:T(2,128)(2,1)S(1)} all-gather(bf16[1,2,1024]{2,1,0:T(2,128)(2,1)S(1)} %bitcast.74), channel_id=1, replica_groups=mesh['dp'=32,'tensor'=8] {'dp'}, dimensions={0}, use_global_device_ids=true | all-gather | bytes 135168 | tf_op jit(solution)/shard_map/all_gather | solution.py:79
  82.7 498.6 %all-gather.7.cloned.1.call-done = bf16[16,430,2048]{2,1,0:T(8,128)(2,1)} async-done(((bf16[2,430,2048]{2,1,0:T(8,128)(2,1)}), bf16[16,430,2048]{2,1,0:T(8,128)(2,1)}) %all-gather.7.cloned.1.call-update) | async-done | bytes 28180496 | tf_op jit(solution)/shard_map/all_gather | solution.py:15
  581.2 13.4 reduce_sum.152
  595.9 14.4 %psum.49 = f32[2,430]{1,0:T(2,128)S(1)} all-reduce(f32[2,430]{1,0:T(2,128)S(1)} %fusion.73), channel_id=1, replica_groups=mesh['dp'=32,'tensor'=8] {'tensor'}, use_global_device_ids=true, to_apply=%region_4.0 | all-reduce | flops 860 | bytes 6880 | tf_op jit(solution)/shard_map/psum | solution.py:69
  611.6 12.6 psum.50
  626.8 14.6 %psum.51 = f32[2,1024]{1,0:T(2,128)S(1)} all-reduce(f32[2,1024]{1,0:T(2,128)S(1)} %fusion.102), channel_id=1, replica_groups=mesh['dp'=32,'tensor'=8] {'tensor'}, use_global_device_ids=true, to_apply=%region_8.0 | all-reduce | flops 2048 | bytes 16384 | tf_op jit(solution)/shard_map/psum | solution.py:76
  644.5 82.7 %all-reduce = (f32[64]{0:T(128)S(1)}, f32[]{:T(128)}) all-reduce(f32[64]{0:T(128)S(1)} %get-tuple-element.30, f32[]{:T(128)S(6)} %sub.68), channel_id=1, replica_groups=mesh['dp'=32,'tensor'=8] {'dp'}, use_global_device_ids=true, to_apply=%region_16.0 | all-reduce | flops 65 | bytes 520 | tf_op jit(solution)/shard_map/psum | solution.py:90
  731.1 12.9 all-reduce.1
  747.7 74.0 %all-gather.5.cloned.1.call-done = bf16[2,430,2048]{2,1,0:T(8,128)(2,1)} async-done(((bf16[2,430,256]{2,1,0:T(8,128)(2,1)}), bf16[2,430,2048]{2,1,0:T(8,128)(2,1)}) %all-gather.5.cloned.1.call-update) | async-done | bytes 3522576 | tf_op jit(solution)/shard_map/all_gather | solution.py:114
  825.0 4.4 fusion.49
  830.0 4.4 fusion.12
  838.5 6.6 fusion.50
  845.7 4.4 fusion.13
  851.6 7.0 fusion.53
  859.2 4.5 fusion.14
  865.1 4.7 fusion.11
  876.8 36.6 %reduce-scatter.17.cloned.1.call-done = bf16[256,32]{0,1:T(8,128)(2,1)} async-done(((bf16[256,1024]{0,1:T(8,128)(2,1)}), bf16[256,32]{0,1:T(8,128)(2,1)}) %reduce-scatter.17.cloned.1.call-update) | async-done | bytes 16400 | tf_op jit(solution)/shard_map/reduce_scatter | solution.py:168
  914.6 89.4 %reduce-scatter.23.cloned.1.call-done = bf16[64,256]{1,0:T(8,128)(2,1)} async-done(((bf16[2048,256]{1,0:T(8,128)(2,1)}), bf16[64,256]{1,0:T(8,128)(2,1)}) %reduce-scatter.23.cloned.1.call-update) | async-done | bytes 32784
  1005.6 89.1 %reduce-scatter.21.cloned.1.call-done = bf16[64,256]{1,0:T(8,128)(2,1)} async-done(((bf16[2048,256]{1,0:T(8,128)(2,1)}), bf16[64,256]{1,0:T(8,128)(2,1)}) %reduce-scatter.21.cloned.1.call-update) | async-done | bytes 32784
  1096.3 89.1 %reduce-scatter.19.cloned.1.call-done = bf16[64,256]{1,0:T(8,128)(2,1)} async-done(((bf16[2048,256]{1,0:T(8,128)(2,1)}), bf16[64,256]{1,0:T(8,128)(2,1)}) %reduce-scatter.19.cloned.1.call-update) | async-done | bytes 32784
  1187.0 89.2 %reduce-scatter.15.cloned.1.call-done = bf16[256,64]{0,1:T(8,128)(2,1)} async-done(((bf16[256,2048]{0,1:T(8,128)(2,1)}), bf16[256,64]{0,1:T(8,128)(2,1)}) %reduce-scatter.15.cloned.1.call-update) | async-done | bytes 32784 | tf_op jit(solution)/shard_map/reduce_scatter | solution.py:165
  1277.6 82.3 %reduce-scatter.13.cloned.1.call-done = bf16[2,430,256]{2,1,0:T(8,128)(2,1)} async-done(((bf16[2,430,2048]{2,1,0:T(8,128)(2,1)}), bf16[2,430,256]{2,1,0:T(8,128)(2,1)}) %reduce-scatter.13.cloned.1.call-update) | async-done | bytes 440336 | tf_op jit(solution)/shard_map/reduce_scatter | solution.py:149
  (100 shorter events, 57.4 us)
Async XLA Ops:
  7.2 21.9 %copy-start = (bf16[256,2048]{1,0:T(8,128)(2,1)S(1)}, bf16[256,2048]{1,0:T(8,128)(2,1)}, u32[]{:S(2)}) copy-start(bf16[256,2048]{1,0:T(8,128)(2,1)} %param.14) | copy-start | bytes 3145732
  7.2 4.7 copy-start.7
  7.2 574.0 %all-gather.7.cloned.1.call-start = ((), (), s32[]{:S(2)}) async-start(), calls=%async_computation.10 | async-start | bytes 31850496 | tf_op jit(solution)/shard_map/all_gather | solution.py:15
  16.7 3.6 copy-start.3
  16.7 4.6 copy-start.2
  16.7 4.8 copy-start.10
  29.1 3.0 copy-start.5
  29.1 3.0 copy-start.13
  29.1 3.0 copy-start.12
  32.0 789.7 %all-gather.5.cloned.1.call-start = ((), (), s32[]{:S(2)}) async-start(), calls=%async_computation.6 | async-start | bytes 3981312 | tf_op jit(solution)/shard_map/all_gather | solution.py:114
  581.2 13.4 copy-start.4
  746.4 166.9 %reduce-scatter.17.cloned.1.call-start = ((), (), s32[]{:S(2)}) async-start(), calls=%async_computation.9 | async-start | bytes 540672 | tf_op jit(solution)/shard_map/reduce_scatter | solution.py:168
  747.7 256.3 %reduce-scatter.23.cloned.1.call-start = ((), (), s32[]{:S(2)}) async-start(), calls=%async_computation.13 | async-start | bytes 1081344
  835.8 258.9 %reduce-scatter.21.cloned.1.call-start = ((), (), s32[]{:S(2)}) async-start(), calls=%async_computation.12 | async-start | bytes 1081344
  851.6 333.8 %reduce-scatter.19.cloned.1.call-start = ((), (), s32[]{:S(2)}) async-start(), calls=%async_computation.11 | async-start | bytes 1081344
  859.2 5.9 copy-start.6
  865.1 5.1 copy-start.8
  865.1 411.2 %reduce-scatter.15.cloned.1.call-start = ((), (), s32[]{:S(2)}) async-start(), calls=%async_computation.8 | async-start | bytes 1081344 | tf_op jit(solution)/shard_map/reduce_scatter | solution.py:165
  869.8 1.4 copy-start.9
  869.9 490.1 %reduce-scatter.13.cloned.1.call-start = ((), (), s32[]{:S(2)}) async-start(), calls=%async_computation.7 | async-start | bytes 3981312 | tf_op jit(solution)/shard_map/reduce_scatter | solution.py:149
  871.3 1.2 copy-start.11
  872.5 489.6 %copy-start.1 = (bf16[256,2048]{1,0:T(8,128)(2,1)S(1)}, bf16[256,2048]{1,0:T(8,128)(2,1)}, u32[]{:S(2)}) copy-start(bf16[256,2048]{1,0:T(8,128)(2,1)} %param.14) | copy-start | bytes 3145732
Sparse Core Ops, SparseCore 0:
  32.1 549.0 all-gather.6
  746.5 75.2 all-gather.4
  825.5 87.7 reduce-scatter.16
  916.9 87.0 reduce-scatter.22
  1007.6 87.0 reduce-scatter.20
  1098.4 86.9 reduce-scatter.18
  1189.2 87.0 reduce-scatter.14
  1278.8 81.0 reduce-scatter.12
